TPU v7x, 512 devices: a whole 4x4x16 slice. The times are simulated.
512 devices in a mesh: var: 16 (over x, z_lo), dp: 32 (over y, z_hi, core).
Axes of the slice: x: 4, y: 4, z: 16 (z_hi: 4, z_lo: 4; z = z_hi * 4 + z_lo), core: 2. Of those that a mesh axis runs over, the one named last changes fastest.
Arguments:
- fields: bfloat16 [32, 64, 32, 128], P('dp', 'var'), may hold values from -6 to 6
- kernels: bfloat16 [64, 16, 512], P('var'), may hold values from -1.5 to 1.5
- level_map: int32 [64], P('var'), may hold values 0 or 1
- norm_gain_vector: float32 [512], replicated, may hold values from 0.1 to 1.9
- w_in: bfloat16 [512, 2048], replicated, may hold values from -0.25 to 0.25
- w_out: bfloat16 [2048, 512], replicated, may hold values from -0.125 to 0.125
- cotangent: bfloat16 [32, 16, 256, 512], P('dp', None, 'var'), may hold values from -6 to 6
Outputs:
- block_out: bfloat16 [32, 16, 256, 512], P('dp', None, 'var')
- kernel_grad: float32 [64, 16, 512], P('var', None, 'dp')
Inputs may be any that keep to these rules, and one draw needn't show every extreme that they name: variable-level v belongs to pressure level v // 4 and enters its aggregate where level_map[v] is 1.
All inputs are finite; a program needn't handle non-finite values. No bound on the sum of `level_map` on one device may be relied on, other than what follows from the above.
Results may differ from a plain program's by a relative error of at most 0.013.
Values may be sent and summed in bfloat16 or wider, within the bound.
No kernel may reach another device: no remote copies, remote signals or barrier semaphores. Data moves between devices by JAX's collectives and lax.ppermute only.
A program may use at most 64 MiB of HBM per device.

v0:
```python
import jax
import jax.numpy as jnp
from jax import lax
from jax.sharding import PartitionSpec as P

PATCH = 4


def patches_of(images):
    batch, count_v, height, width = images.shape
    shaped = images.reshape(batch, count_v, height // PATCH, PATCH, width // PATCH, PATCH)
    return shaped.transpose(0, 1, 2, 4, 3, 5).reshape(
        batch, count_v, height // PATCH * (width // PATCH), PATCH * PATCH
    )


def block_pass(token_rows, grads, norm_gain_vector, w_in, w_out):
    width = token_rows.shape[-1]
    rows = token_rows.reshape(-1, width).astype(jnp.float32)
    mean_row = jnp.mean(rows, axis=1, keepdims=True)
    centered_rows = rows - mean_row
    reciprocal_std = lax.rsqrt(
        jnp.mean(centered_rows * centered_rows, axis=1, keepdims=True) + 1e-05
    )
    normalized_input = centered_rows * reciprocal_std
    normalized_rows = (normalized_input * norm_gain_vector).astype(jnp.bfloat16)
    pre = jnp.dot(normalized_rows, w_in, preferred_element_type=jnp.float32)
    hidden = jax.nn.gelu(pre, approximate=True).astype(jnp.bfloat16)
    output = (rows + jnp.dot(hidden, w_out, preferred_element_type=jnp.float32)).astype(
        jnp.bfloat16
    )
    gradient_rows = grads.reshape(-1, width)
    dhid = jnp.dot(gradient_rows, w_out.T, preferred_element_type=jnp.float32)
    gelu_back = jax.vjp(lambda value: jax.nn.gelu(value, approximate=True), pre)[1]
    dpre = gelu_back(dhid)[0].astype(jnp.bfloat16)
    dnorm = jnp.dot(dpre, w_in.T, preferred_element_type=jnp.float32)
    normalized_gradient = dnorm * norm_gain_vector
    token_gradient = gradient_rows.astype(jnp.float32) + reciprocal_std * (
        normalized_gradient
        - jnp.mean(normalized_gradient, axis=1, keepdims=True)
        - normalized_input * jnp.mean(normalized_gradient * normalized_input, axis=1, keepdims=True)
    )
    return (
        output.reshape(token_rows.shape),
        token_gradient.astype(jnp.bfloat16).reshape(token_rows.shape),
    )


def level_tables(level, weight, groups):
    onehot = (level[None, :] == jnp.arange(groups, dtype=jnp.int32)[:, None]).astype(
        jnp.float32
    ) * weight[None, :]
    inv = 1.0 / jnp.maximum(jnp.sum(onehot, axis=1), 1.0)
    return (onehot * inv[:, None], inv[level] * weight)


def local(fields, kernels, level_map, norm_gain_vector, w_in, w_out, cotangent):
    batch, var_local = (fields.shape[0], fields.shape[1])
    patch_inputs = patches_of(fields)
    tokens_all = patch_inputs.shape[2]
    scale = float(batch * lax.axis_size("dp") * tokens_all) ** (-0.5)
    own_level = jnp.zeros((var_local,), jnp.int32)
    own_assign, own_member = level_tables(own_level, level_map.astype(jnp.float32), 1)
    patch_embeddings = jnp.einsum(
        "bvnp,vpe->bvne", patch_inputs, kernels, preferred_element_type=jnp.float32
    )
    token_rows = jnp.einsum("lv,bvne->blne", own_assign, patch_embeddings).astype(jnp.bfloat16)
    row_tokens = lax.all_to_all(token_rows, "var", split_axis=2, concat_axis=1, tiled=True)
    block_out, token_gradient = block_pass(row_tokens, cotangent, norm_gain_vector, w_in, w_out)
    dlevel = lax.all_to_all(token_gradient, "var", split_axis=1, concat_axis=2, tiled=True)
    partial_grad = (
        jnp.einsum("bvnp,bne->vpe", patch_inputs, dlevel[:, 0], preferred_element_type=jnp.float32)
        * own_member[:, None, None]
    )
    kernel_grad = lax.psum_scatter(partial_grad, "dp", scatter_dimension=2, tiled=True) * scale
    return (block_out, kernel_grad)


def solution(mesh):
    placed = (
        P("dp", "var", None, None),
        P("var", None, None),
        P("var"),
        P(),
        P(),
        P(),
        P("dp", None, "var", None),
    )
    return jax.shard_map(
        local,
        mesh=mesh,
        in_specs=placed,
        out_specs=(P("dp", None, "var", None), P("var", None, "dp")),
        check_vma=False,
    )
```

profile of v0, /device:TPU:2, one launch (start us, length us, event | category | flops | bytes accessed | tf_op | source)
XLA Modules:
  0.0 183.3 jit_solution(2640362188607401655)
XLA Ops:
  7.2 0.0 copy-start
  7.2 1.4 convert_reduce_fusion.1
  9.3 3.0 %reshape.106 = bf16[1,4,8,4,32,4]{5,4,3,2,1,0:T(8,128)(2,1)S(1)} reshape(bf16[1,4,32,128]{3,2,1,0:T(8,128)(2,1)} %param.7) | data formatting | bytes 65536 | tf_op jit(solution)/shard_map/reshape | solution.py:11
  12.3 0.9 copy.14
  13.2 0.1 reshape.107
  13.3 0.5 convolution_bitcast_fusion
  13.8 1.8 copy.18
  15.6 1.9 %fusion.47 = bf16[1,256,512]{2,0,1:T(2,128)(2,1)S(1)} fusion(bf16[4,256,512]{2,0,1:T(4,128)(2,1)} %copy.18, f32[]{:T(128)S(6)} %div.16, s32[4]{0:T(128)S(1)} %copy-done.4), kind=kOutput, calls=%fused_computation.62 | convolution fusion | flops 1048584 | bytes 1310740 | tf_op jit(solution)/shard_map/lv,bvne->blne/dot_general | solution.py:67
  17.6 0.4 copy.28
  18.0 0.5 broadcast.100
  18.5 2.3 %reduce.6 = bf16[256,512]{1,0:T(8,128)(2,1)S(1)} reduce(bf16[256,1,1,512]{3,2,1,0:T(2,128)(2,1)S(1)} %bitcast.92, bf16[]{:T(256)} %broadcast.100), dimensions={1,2}, to_apply=%bitcast.88.reduce_sub_computation | reduce | bytes 524290
  20.8 0.2 reshape.120
  21.0 17.0 %all_to_all.8 = bf16[16,2,4096]{2,1,0:T(2,128)(2,1)S(1)} all-to-all(bf16[16,2,4096]{2,1,0:T(2,128)(2,1)S(1)} %reshape.120), channel_id=1, replica_groups=mesh['var'=16,'dp'=32] {'var'}, dimensions={0} | all-to-all | bytes 524288 | tf_op jit(solution)/shard_map/all_to_all | solution.py:68
  38.0 0.3 reshape.121
  38.3 0.1 convert_reduce_fusion
  38.4 0.2 fusion.24
  38.7 2.1 %fusion.26 = f32[256,2048]{1,0:T(8,128)} fusion(bf16[512,2048]{1,0:T(8,128)(2,1)S(1)} %copy-done, bf16[1,1,256,512]{3,2,1,0:T(8,128)(2,1)S(1)} %get-tuple-element.5, f32[512]{0:T(512)S(1)} %copy-done.3, f32[256]{0:T(256)S(1)} %add_rsqrt_fusion, f32[256]{0:T(256)S(1)} %broadcast_multiply_fusion.3), kind=kOutput, calls=%fused_computation.35 | convolution fusion | flops 537526272 | bytes 4460544 | tf_op jit(solution)/shard_map/dot_general | solution.py:27
  40.8 4.7 %fusion.43 = (f32[256]{0:T(256)S(1)}, f32[256]{0:T(256)S(1)}, f32[256,512]{1,0:T(8,128)S(1)}) fusion(f32[256]{0:T(256)S(1)} %add_rsqrt_fusion, f32[256]{0:T(256)S(1)} %broadcast_multiply_fusion.3, bf16[1,1,256,512]{3,2,1,0:T(8,128)(2,1)S(1)} %get-tuple-element.5, f32[512]{0:T(512)S(1)} %copy-done.3, bf16[512,2048]{1,0:T(8,128)(2,1)S(1)} %copy-done, ...), kind=kOutput, calls=%fused_computation.59 | convolution fusion | flops 1085144576 | bytes 7346176 | tf_op jit(solution)/shard_map/dot_general | solution.py:36
  45.5 1.0 fusion.22
  46.4 6.0 %all-to-all-start.1 = ((bf16[1,16,16,512]{3,2,0,1:T(8,128)(2,1)}), bf16[1,16,16,512]{3,2,0,1:T(8,128)(2,1)S(1)}, u32[]{:S(2)}, u32[]{:S(2)}) async-start(bf16[1,16,16,512]{3,2,0,1:T(8,128)(2,1)} %bitcast.11), calls=%async_computation.1 | async-start | bytes 524288 | tf_op jit(solution)/shard_map/all_to_all | solution.py:70
  52.5 0.0 reduce-scatter.4.cloned.1.call-start
  52.5 7.6 %all-to-all-done.1 = bf16[1,16,16,512]{3,2,0,1:T(8,128)(2,1)S(1)} async-done(((bf16[1,16,16,512]{3,2,0,1:T(8,128)(2,1)}), bf16[1,16,16,512]{3,2,0,1:T(8,128)(2,1)S(1)}, u32[]{:S(2)}, u32[]{:S(2)}) %all-to-all-start.1) | async-done | bytes 262176 | tf_op jit(solution)/shard_map/all_to_all | solution.py:70
  60.1 0.2 fusion.50
  60.3 0.1 multiply_bitcast_fusion
  60.4 0.4 copy.20
  60.8 1.2 reshape.118
  62.0 0.0 reduce-scatter.4.cloned.1.call-update
  62.0 3.8 %fusion.7 = bf16[256,512]{1,0:T(8,128)(2,1)} fusion(bf16[2048,512]{1,0:T(8,128)(2,1)} %param.12, f32[256,2048]{1,0:T(8,128)} %fusion.26, bf16[1,1,256,512]{3,2,1,0:T(8,128)(2,1)S(1)} %get-tuple-element.5), kind=kOutput, calls=%fused_computation.13 | convolution fusion | flops 541982720 | bytes 4718592 | tf_op jit(solution)/shard_map/dot_general | solution.py:29
  65.7 109.2 %reduce-scatter.4.cloned.1.call-done = f32[16,64]{1,0:T(8,128)} async-done(((f32[512,64]{1,0:T(8,128)}), f32[16,64]{1,0:T(8,128)}) %reduce-scatter.4.cloned.1.call-update) | async-done | bytes 4112
  175.0 0.8 reshape.119
  175.8 0.1 copy.21
  175.8 0.6 broadcast_multiply_fusion
  (14 shorter events, 0.1 us)
Async XLA Ops:
  7.2 31.5 %copy-start = (bf16[512,2048]{1,0:T(8,128)(2,1)S(1)}, bf16[512,2048]{1,0:T(8,128)(2,1)}, u32[]{:S(2)}) copy-start(bf16[512,2048]{1,0:T(8,128)(2,1)} %param.11) | copy-start | bytes 6291460
  7.2 6.1 %copy-start.2 = (bf16[4,16,512]{2,1,0:T(8,128)(2,1)S(1)}, bf16[4,16,512]{2,1,0:T(8,128)(2,1)}, u32[]{:S(2)}) copy-start(bf16[4,16,512]{2,1,0:T(8,128)(2,1)} %param.8) | copy-start | bytes 196612
  12.3 3.3 %copy-start.4 = (s32[4]{0:T(128)S(1)}, s32[4]{0:T(128)}, u32[]{:S(2)}) copy-start(s32[4]{0:T(128)} %param.9) | copy-start | bytes 52
  17.6 21.0 %copy-start.3 = (f32[512]{0:T(512)S(1)}, f32[512]{0:T(512)}, u32[]{:S(2)}) copy-start(f32[512]{0:T(512)} %param.10) | copy-start | bytes 6148
  38.7 2.2 %copy-start.1 = (bf16[1,16,16,512]{3,2,1,0:T(8,128)(2,1)S(1)}, bf16[1,16,16,512]{3,2,1,0:T(8,128)(2,1)}, u32[]{:S(2)}) copy-start(bf16[1,16,16,512]{3,2,1,0:T(8,128)(2,1)} %param.13) | copy-start | bytes 786436
  46.4 13.7 %all-to-all-start.1 = ((bf16[1,16,16,512]{3,2,0,1:T(8,128)(2,1)}), bf16[1,16,16,512]{3,2,0,1:T(8,128)(2,1)S(1)}, u32[]{:S(2)}, u32[]{:S(2)}) async-start(bf16[1,16,16,512]{3,2,0,1:T(8,128)(2,1)} %bitcast.11), calls=%async_computation.1 | async-start | bytes 524288 | tf_op jit(solution)/shard_map/all_to_all | solution.py:70
  52.5 122.5 %reduce-scatter.4.cloned.1.call-start = ((), (), s32[]{:S(2)}) async-start(), calls=%async_computation.3 | async-start | bytes 270336
Sparse Core Ops, SparseCore 0:
  62.1 112.8 reduce-scatter.3
where the time goes:
time: 184 us; the launch traced here: 183 us
  waiting for transfers between devices  117 us (64%)
  blocking collectives  17 us (9%)
  between operations  14.9 us (8%)
  matrix products  13.1 us (7%)
  local copies, waits for them, and re-layouts  9.68 us (5%)
  starting transfers between devices  6.06 us (3%)
  other arithmetic  5.72 us (3%)
    unnamed x2, waiting for transfers between devices  109 us
    all_to_all x1, blocking collectives, local(): lax.all_to_all(token_rows, 'var', split_axis=2, concat_axis=1, tiled=True)  17 us
    all_to_all x1, waiting for transfers between devices, local(): lax.all_to_all(token_gradient, 'var', split_axis=1, concat_axis=2, tiled=...  7.6 us
    all_to_all x1, starting transfers between devices, local(): lax.all_to_all(token_gradient, 'var', split_axis=1, concat_axis=2, tiled=...  6.03 us
    dot_general x1, matrix products, block_pass(): dnorm = jnp.dot(dpre, w_in.T, preferred_element_type=jnp.float32)  4.66 us
    dot_general x1, matrix products, block_pass(): jnp.dot(hidden, w_out, preferred_element_type=jnp.float32)  3.76 us
  transfers between devices with their start and end apart: 2, of which 2 were waited for; matrix products, arithmetic and copies ran while one was open for 2% of the time, Pallas kernels for 0%

commit v1 on v0

--- a/solution.py
+++ b/solution.py
@@ -2,6 +2,7 @@
 import jax.numpy as jnp
 from jax import lax
 from jax.sharding import PartitionSpec as P
+from jax.lax import all_to_all, axis_size
 
 PATCH = 4
 
@@ -67,7 +68,19 @@
     token_rows = jnp.einsum("lv,bvne->blne", own_assign, patch_embeddings).astype(jnp.bfloat16)
     row_tokens = lax.all_to_all(token_rows, "var", split_axis=2, concat_axis=1, tiled=True)
     block_out, token_gradient = block_pass(row_tokens, cotangent, norm_gain_vector, w_in, w_out)
-    dlevel = lax.all_to_all(token_gradient, "var", split_axis=1, concat_axis=2, tiled=True)
+
+    def prepare_outputs(v0):
+        return jnp.concatenate(
+            all_to_all(
+                jnp.stack(jnp.split(v0, axis_size("var"), axis=1), axis=0),
+                axis_name="var",
+                split_axis=0,
+                concat_axis=0,
+            ),
+            2,
+        )
+
+    dlevel = prepare_outputs(token_gradient)
     partial_grad = (
         jnp.einsum("bvnp,bne->vpe", patch_inputs, dlevel[:, 0], preferred_element_type=jnp.float32)
         * own_member[:, None, None]

time: 184 us -> 193 us (1.049)
  local copies, waits for them, and re-layouts: 9.68 us -> 19.4 us
    unnamed x17 -> x32, local copies, waits for them, and re-layouts: 3.43 us -> 12.5 us
where the time goes in v1:
time: 193 us; the launch traced here: 192 us
  waiting for transfers between devices  117 us (61%)
  local copies, waits for them, and re-layouts  19.4 us (10%)
  blocking collectives  17 us (9%)
  between operations  14.9 us (8%)
  matrix products  13.1 us (7%)
  starting transfers between devices  6.04 us (3%)
  other arithmetic  4.95 us (3%)
    unnamed x2, waiting for transfers between devices  109 us
    all_to_all x1, blocking collectives, local(): lax.all_to_all(token_rows, 'var', split_axis=2, concat_axis=1, tiled=True)  17 us
    unnamed x32, local copies, waits for them, and re-layouts  12.5 us
    all_to_all x1, waiting for transfers between devices, prepare_outputs(): all_to_all(jnp.stack(jnp.split(v0, axis_size('var'), axis=1), axis=0), ax...  7.61 us
    all_to_all x1, starting transfers between devices, prepare_outputs(): all_to_all(jnp.stack(jnp.split(v0, axis_size('var'), axis=1), axis=0), ax...  6 us
    dot_general x1, matrix products, block_pass(): dnorm = jnp.dot(dpre, w_in.T, preferred_element_type=jnp.float32)  4.64 us
  transfers between devices with their start and end apart: 2, of which 2 were waited for; matrix products, arithmetic and copies ran while one was open for 2% of the time, Pallas kernels for 0%

profile of v1, /device:TPU:2, one launch (start us, length us, event | category | flops | bytes accessed | tf_op | source)
XLA Modules:
  0.0 192.3 jit_solution(17683489372025153229)
XLA Ops:
  7.2 1.4 convert_reduce_fusion.1
  9.3 3.0 %reshape.102 = bf16[1,4,8,4,32,4]{5,4,3,2,1,0:T(8,128)(2,1)S(1)} reshape(bf16[1,4,32,128]{3,2,1,0:T(8,128)(2,1)} %param.7) | data formatting | bytes 65536 | tf_op jit(solution)/shard_map/reshape | solution.py:12
  12.3 0.9 copy.13
  13.8 1.8 copy.16
  15.6 1.9 fusion.47
  18.5 2.2 %reduce.6 = bf16[256,512]{1,0:T(8,128)(2,1)S(1)} reduce(bf16[256,1,1,512]{3,2,1,0:T(2,128)(2,1)S(1)} %bitcast.154, bf16[]{:T(256)} %broadcast.100), dimensions={1,2}, to_apply=%bitcast.150.reduce_sub_computation | reduce | bytes 524290
  20.9 17.0 %all_to_all.14 = bf16[16,2,4096]{2,1,0:T(2,128)(2,1)S(1)} all-to-all(bf16[16,2,4096]{2,1,0:T(2,128)(2,1)S(1)} %reshape.116), channel_id=1, replica_groups=mesh['var'=16,'dp'=32] {'var'}, dimensions={0} | all-to-all | bytes 524288 | tf_op jit(solution)/shard_map/all_to_all | solution.py:69
  38.6 2.2 %fusion.26 = f32[256,2048]{1,0:T(8,128)} fusion(bf16[512,2048]{1,0:T(8,128)(2,1)S(1)} %copy-done, bf16[1,1,256,512]{3,2,1,0:T(8,128)(2,1)S(1)} %get-tuple-element.5, f32[512]{0:T(512)S(1)} %copy-done.3, f32[256]{0:T(256)S(1)} %add_rsqrt_fusion, f32[256]{0:T(256)S(1)} %broadcast_multiply_fusion.3), kind=kOutput, calls=%fused_computation.35 | convolution fusion | flops 537526272 | bytes 4460544 | tf_op jit(solution)/shard_map/dot_general | solution.py:28
  40.8 4.6 %fusion.43 = (f32[256]{0:T(256)S(1)}, f32[256]{0:T(256)S(1)}, f32[256,512]{1,0:T(8,128)S(1)}) fusion(f32[256]{0:T(256)S(1)} %add_rsqrt_fusion, f32[256]{0:T(256)S(1)} %broadcast_multiply_fusion.3, bf16[1,1,256,512]{3,2,1,0:T(8,128)(2,1)S(1)} %get-tuple-element.5, f32[512]{0:T(512)S(1)} %copy-done.3, bf16[512,2048]{1,0:T(8,128)(2,1)S(1)} %copy-done, ...), kind=kOutput, calls=%fused_computation.91 | convolution fusion | flops 1085144576 | bytes 7346176 | tf_op jit(solution)/shard_map/dot_general | solution.py:37
  45.7 0.6 constant_dynamic-update-slice_fusion.15
  46.3 0.6 constant_dynamic-update-slice_fusion.14
  46.9 0.6 constant_dynamic-update-slice_fusion.13
  47.5 0.6 constant_dynamic-update-slice_fusion.12
  48.1 0.6 constant_dynamic-update-slice_fusion.11
  48.7 0.6 constant_dynamic-update-slice_fusion.10
  49.3 0.6 constant_dynamic-update-slice_fusion.9
  49.9 0.6 constant_dynamic-update-slice_fusion.8
  50.5 0.6 constant_dynamic-update-slice_fusion.7
  51.1 0.6 constant_dynamic-update-slice_fusion.6
  51.7 0.6 constant_dynamic-update-slice_fusion.5
  52.4 0.6 constant_dynamic-update-slice_fusion.4
  53.0 0.6 constant_dynamic-update-slice_fusion.3
  53.6 0.6 constant_dynamic-update-slice_fusion.2
  54.2 0.6 constant_dynamic-update-slice_fusion.1
  54.8 0.6 constant_dynamic-update-slice_fusion
  55.4 6.0 %all-to-all-start.1 = ((bf16[16,1,1,16,512]{4,3,2,1,0:T(8,128)(2,1)}), bf16[16,1,1,16,512]{4,3,2,1,0:T(8,128)(2,1)S(1)}, u32[]{:S(2)}, u32[]{:S(2)}) async-start(bf16[16,1,1,16,512]{4,3,2,1,0:T(8,128)(2,1)} %constant_dynamic-update-slice_fusion), calls=%async_computation.1 | async-start | bytes 524288 | tf_op jit(solution)/shard_map/all_to_all | solution.py:74
  61.4 7.6 %all-to-all-done.1 = bf16[16,1,1,16,512]{4,3,2,1,0:T(8,128)(2,1)S(1)} async-done(((bf16[16,1,1,16,512]{4,3,2,1,0:T(8,128)(2,1)}), bf16[16,1,1,16,512]{4,3,2,1,0:T(8,128)(2,1)S(1)}, u32[]{:S(2)}, u32[]{:S(2)}) %all-to-all-start.1) | async-done | bytes 262176 | tf_op jit(solution)/shard_map/all_to_all | solution.py:74
  69.7 1.2 reshape.114
  70.9 3.8 %fusion.7 = bf16[256,512]{1,0:T(8,128)(2,1)} fusion(bf16[2048,512]{1,0:T(8,128)(2,1)} %param.12, f32[256,2048]{1,0:T(8,128)} %fusion.26, bf16[1,1,256,512]{3,2,1,0:T(8,128)(2,1)S(1)} %get-tuple-element.5), kind=kOutput, calls=%fused_computation.13 | convolution fusion | flops 541982720 | bytes 4718592 | tf_op jit(solution)/shard_map/dot_general | solution.py:30
  74.7 109.3 %reduce-scatter.4.cloned.1.call-done = f32[16,64]{1,0:T(8,128)} async-done(((f32[512,64]{1,0:T(8,128)}), f32[16,64]{1,0:T(8,128)}) %reduce-scatter.4.cloned.1.call-update) | async-done | bytes 4112
  183.9 0.8 reshape.115
  184.8 0.6 broadcast_multiply_fusion
  (30 shorter events, 3.4 us)
Async XLA Ops:
  7.2 31.4 %copy-start = (bf16[512,2048]{1,0:T(8,128)(2,1)S(1)}, bf16[512,2048]{1,0:T(8,128)(2,1)}, u32[]{:S(2)}) copy-start(bf16[512,2048]{1,0:T(8,128)(2,1)} %param.11) | copy-start | bytes 6291460
  7.2 6.1 %copy-start.2 = (bf16[4,16,512]{2,1,0:T(8,128)(2,1)S(1)}, bf16[4,16,512]{2,1,0:T(8,128)(2,1)}, u32[]{:S(2)}) copy-start(bf16[4,16,512]{2,1,0:T(8,128)(2,1)} %param.8) | copy-start | bytes 196612
  12.3 3.3 %copy-start.4 = (s32[4]{0:T(128)S(1)}, s32[4]{0:T(128)}, u32[]{:S(2)}) copy-start(s32[4]{0:T(128)} %param.9) | copy-start | bytes 52
  17.6 21.0 %copy-start.3 = (f32[512]{0:T(512)S(1)}, f32[512]{0:T(512)}, u32[]{:S(2)}) copy-start(f32[512]{0:T(512)} %param.10) | copy-start | bytes 6148
  38.6 2.2 %copy-start.1 = (bf16[1,16,16,512]{3,2,1,0:T(8,128)(2,1)S(1)}, bf16[1,16,16,512]{3,2,1,0:T(8,128)(2,1)}, u32[]{:S(2)}) copy-start(bf16[1,16,16,512]{3,2,1,0:T(8,128)(2,1)} %param.13) | copy-start | bytes 786436
  55.4 13.7 %all-to-all-start.1 = ((bf16[16,1,1,16,512]{4,3,2,1,0:T(8,128)(2,1)}), bf16[16,1,1,16,512]{4,3,2,1,0:T(8,128)(2,1)S(1)}, u32[]{:S(2)}, u32[]{:S(2)}) async-start(bf16[16,1,1,16,512]{4,3,2,1,0:T(8,128)(2,1)} %constant_dynamic-update-slice_fusion), calls=%async_computation.1 | async-start | bytes 524288 | tf_op jit(solution)/shard_map/all_to_all | solution.py:74
  61.4 122.6 %reduce-scatter.4.cloned.1.call-start = ((), (), s32[]{:S(2)}) async-start(), calls=%async_computation.3 | async-start | bytes 270336
Sparse Core Ops, SparseCore 0:
  71.0 112.8 reduce-scatter.3
